TPU v7x, 512 devices: a whole 4x4x16 slice. The times are simulated.
512 devices in a mesh: req: 64 (over y_hi, z, core), tp: 8 (over y_lo, x).
Axes of the slice: x: 4, y: 4 (y_hi: 2, y_lo: 2; y = y_hi * 2 + y_lo), z: 16, core: 2. Of those that a mesh axis runs over, the one named last changes fastest.
Arguments:
- tokens: bfloat16 [64, 512, 2048], P('req', 'tp'), may hold values from -6 to 6
- w_q: bfloat16 [2048, 1024], P(None, 'tp')
- w_k: bfloat16 [2048, 1024], P(None, 'tp')
- w_v: bfloat16 [2048, 1024], P(None, 'tp'), may hold values from -0.125 to 0.125
- w_o: bfloat16 [1024, 2048], P('tp'), may hold values from -0.1875 to 0.1875
- q_gain: float32 [1024], P('tp'), may hold values from 0.1 to 1.9
- k_gain: float32 [1024], P('tp'), may hold values from 0.1 to 1.9
- out_gain: float32 [2048], replicated, may hold values from 0.1 to 1.9
- cache_lens: int32 [64], P('req'), may hold values from 512 to 4096, as said below
- group_ids: int32 [64], replicated, may hold values from 0 to 7
- prefix_cache: bfloat16 [8, 1024, 2048], P(None, 'req', 'tp'), may hold values from -6 to 6
- cache_rows: bfloat16 [64, 4096, 2048], P('req', None, 'tp'), may hold values from -105 to 105
Outputs:
- hidden: bfloat16 [64, 512, 2048], P('req', 'tp')
- appended: bfloat16 [64, 512, 2048], P('req', None, 'tp')
Inputs may be any that keep to these rules, and one draw needn't show every extreme that they name: `cache_lens`: every draw holds a request with exactly 4096 cached positions.
All inputs are finite; a program needn't handle non-finite values.
Results may differ from a plain program's by a relative error of at most 0.013.
Values may be sent and summed in bfloat16 or wider, within the bound.
No kernel may reach another device: no remote copies, remote signals or barrier semaphores. Data moves between devices by JAX's collectives and lax.ppermute only.
A program may use at most 64 MiB of HBM per device.

v0:
```python
import jax
import jax.numpy as jnp
from jax import lax
from jax.sharding import PartitionSpec as P

HEADS = 8
HD = 128
NEW = 512


def rotate(values_in, positions):
    half_dim = values_in.shape[-1] // 2
    exponent = jnp.arange(half_dim, dtype=jnp.float32) * (-2.0 / values_in.shape[-1])
    inverse = jnp.power(jnp.float32(500000.0), exponent)
    angles = positions[:, None] * inverse[None, :]
    cosine = jnp.cos(angles)[:, None, :]
    sine_part = jnp.sin(angles)[:, None, :]
    first_half = values_in[..., :half_dim]
    second_half = values_in[..., half_dim:]
    return jnp.concatenate(
        [
            first_half * cosine - second_half * sine_part,
            second_half * cosine + first_half * sine_part,
        ],
        -1,
    )


def rms_scale(values_in, gain_vector):
    mean_sq = jnp.mean(values_in * values_in, axis=-1, keepdims=True)
    return values_in * lax.rsqrt(mean_sq + 1e-06) * gain_vector


def absorb(state_now, queries, keys_block, values_block, visible):
    running_max, denominator, weighted = state_now
    scores = jnp.einsum(
        "hqd,khd->hqk", queries, keys_block, preferred_element_type=jnp.float32
    ) * HD ** (-0.5)
    scores = jnp.where(visible[None], scores, -1e30)
    updated = jnp.maximum(running_max, jnp.max(scores, -1))
    factor = jnp.exp(running_max - updated)
    weights = jnp.where(visible[None], jnp.exp(scores - updated[..., None]), 0.0)
    denominator = denominator * factor + jnp.sum(weights, -1)
    weighted = weighted * factor[..., None] + jnp.einsum(
        "hqk,khd->hqd",
        weights.astype(jnp.bfloat16),
        values_block,
        preferred_element_type=jnp.float32,
    )
    return (updated, denominator, weighted)


def per_device(
    tokens,
    w_q,
    w_k,
    w_v,
    w_o,
    q_gain,
    k_gain,
    out_gain,
    cache_lens,
    group_ids,
    prefix_cache,
    cache_rows,
):
    heads_local = w_q.shape[1] // HD
    width_local = heads_local * HD
    flat_rows = lax.all_gather(tokens, "tp", axis=1, tiled=True)[0]
    projected = jnp.concatenate(
        [
            jnp.dot(flat_rows, w_q, preferred_element_type=jnp.float32)[None],
            jnp.dot(flat_rows, w_k, preferred_element_type=jnp.float32)[None],
            jnp.dot(flat_rows, w_v, preferred_element_type=jnp.float32)[None],
        ],
        axis=2,
    )[0]
    queries = projected[:, :width_local]
    keys_new = projected[:, width_local : 2 * width_local]
    values_new = projected[:, 2 * width_local :]
    square_sums = lax.psum((jnp.sum(queries * queries, -1), jnp.sum(keys_new * keys_new, -1)), "tp")
    full_width = HEADS * HD
    queries = queries * lax.rsqrt(square_sums[0] / full_width + 1e-06)[:, None] * q_gain
    keys_new = keys_new * lax.rsqrt(square_sums[1] / full_width + 1e-06)[:, None] * k_gain
    prefix_len = prefix_cache.shape[1] * lax.axis_size("req")
    length = cache_lens[0]
    positions = (prefix_len + length + jnp.arange(NEW, dtype=jnp.int32)).astype(jnp.float32)
    q_rot = rotate(queries.reshape(NEW, heads_local, HD), positions).astype(jnp.bfloat16)
    k_rot = rotate(keys_new.reshape(NEW, heads_local, HD), positions).astype(jnp.bfloat16)
    v_new = values_new.reshape(NEW, heads_local, HD).astype(jnp.bfloat16)
    appended = jnp.stack([k_rot, v_new], axis=2).reshape(1, NEW, heads_local * 2 * HD)
    q_heads = jnp.transpose(q_rot, (1, 0, 2))
    state_now = (
        jnp.full((heads_local, NEW), -1e30, jnp.float32),
        jnp.zeros((heads_local, NEW), jnp.float32),
        jnp.zeros((heads_local, NEW, HD), jnp.float32),
    )
    row_ids = jnp.arange(NEW, dtype=jnp.int32)
    state_now = absorb(state_now, q_heads, k_rot, v_new, row_ids[None, :] <= row_ids[:, None])
    cached = cache_rows[0]
    key_block = min(512, cached.shape[0])

    def cache_step(block_index, state_in):
        block = lax.dynamic_slice_in_dim(cached, block_index * key_block, key_block, 0).reshape(
            key_block, heads_local, 2, HD
        )
        columns = block_index * key_block + jnp.arange(key_block, dtype=jnp.int32)
        visible = jnp.broadcast_to(columns[None, :] < length, (NEW, key_block))
        return absorb(state_in, q_heads, block[:, :, 0], block[:, :, 1], visible)

    block_count = cached.shape[0] // key_block
    state_now = lax.fori_loop(0, block_count, cache_step, state_now)
    group_id = group_ids[lax.axis_index("req")]
    chosen = lax.dynamic_index_in_dim(
        lax.all_gather(prefix_cache, "req", axis=1, tiled=True), group_id, 0, keepdims=False
    )
    count = chosen.shape[0]
    chosen = chosen.reshape(count, heads_local, 2, HD)
    state_now = absorb(
        state_now, q_heads, chosen[:, :, 0], chosen[:, :, 1], jnp.ones((NEW, count), dtype=bool)
    )
    running_max, denominator, weighted = state_now
    attended = (
        jnp.transpose(weighted / denominator[..., None], (1, 0, 2))
        .reshape(NEW, width_local)
        .astype(jnp.bfloat16)
    )
    partial_out = jnp.dot(attended, w_o, preferred_element_type=jnp.float32)
    share_rows = tokens.shape[1]
    summed = lax.psum(partial_out.astype(jnp.bfloat16), "tp").astype(jnp.float32)
    mine = lax.dynamic_slice_in_dim(summed, lax.axis_index("tp") * share_rows, share_rows, 0)
    hidden = (tokens[0].astype(jnp.float32) + rms_scale(mine, out_gain)).astype(jnp.bfloat16)[None]
    return (hidden, appended)


def solution(mesh):
    return jax.shard_map(
        per_device,
        mesh=mesh,
        in_specs=(
            P("req", "tp", None),
            P(None, "tp"),
            P(None, "tp"),
            P(None, "tp"),
            P("tp", None),
            P("tp"),
            P("tp"),
            P(),
            P("req"),
            P(),
            P(None, "req", "tp"),
            P("req", None, "tp"),
        ),
        out_specs=(P("req", "tp", None), P("req", None, "tp")),
        check_vma=False,
    )
```

profile of v0, /device:TPU:32, one launch (start us, length us, event | category | flops | bytes accessed | tf_op | source)
XLA Modules:
  0.0 328.0 jit_solution(8489403628430038322)
XLA Ops:
  7.2 0.7 all-gather.3.cloned.1.call-update
  8.0 1.5 copy.30
  10.2 3.0 copy.28
  13.2 0.6 dynamic_slice.17
  15.8 47.3 %all-gather.3.cloned.1.call-done = bf16[1,512,2048]{2,1,0:T(8,128)(2,1)} async-done(((bf16[1,64,2048]{2,1,0:T(8,128)(2,1)}), bf16[1,512,2048]{2,1,0:T(8,128)(2,1)}) %all-gather.3.cloned.1.call-update) | async-done | bytes 2097168 | tf_op jit(solution)/shard_map/all_gather | solution.py:69
  63.1 2.6 fusion.19
  65.7 0.8 fusion.22
  66.5 0.2 copy-done.8
  66.7 0.8 fusion.25
  67.5 0.1 maximum_bitcast_fusion
  67.6 0.1 multiply_reduce_fusion.1
  67.7 17.2 %all-reduce = (f32[512]{0:T(512)S(1)}, f32[512]{0:T(512)S(1)}) all-reduce(f32[512]{0:T(512)S(1)} %get-tuple-element.168, f32[512]{0:T(512)S(1)} %get-tuple-element.167), channel_id=1, replica_groups=mesh['req'=64,'tp'=8] {'tp'}, use_global_device_ids=true, to_apply=%region_1.0 | all-reduce | flops 1024 | bytes 8192 | tf_op jit(solution)/shard_map/psum | solution.py:81
  84.9 0.1 multiply_bitcast_fusion
  85.0 1.3 fusion.63
  86.2 0.6 copy-done.4
  86.9 1.5 pad_maximum_fusion.2
  88.4 1.0 copy.29
  89.4 1.3 fusion.78
  90.7 0.2 fusion.39
  90.9 1.3 fusion.28
  92.2 15.0 %while.17 = (s32[]{:T(128)}, f32[1,512]{1,0:T(1,128)S(1)}, f32[1,512]{1,0:T(1,128)S(1)}, f32[1,512,128]{2,1,0:T(8,128)S(1)}, s32[]{:T(128)}, /*index=5*/bf16[409...) while((s32[]{:T(128)}, f32[1,512]{1,0:T(1,128)S(1)}, ...), condition=%wide.region_9.10_spmd, body=%wide.region_6.9_spmd.sunk | while | flops 136710144 | bytes 4622503 | solution.py:112
  92.2 0.7 add_compare_fusion.2
  92.9 0.3 fusion.88
  93.2 0.2 fusion.89
  93.5 0.6 fusion.90
  94.1 0.7 add_compare_fusion.2
  94.8 0.3 fusion.88
  95.1 0.2 fusion.89
  95.3 0.6 fusion.90
  96.0 0.7 add_compare_fusion.2
  96.6 0.3 fusion.88
  97.0 0.2 fusion.89
  97.2 0.6 fusion.90
  97.8 0.7 add_compare_fusion.2
  98.5 0.3 fusion.88
  98.9 0.2 fusion.89
  99.1 0.6 fusion.90
  99.7 0.7 add_compare_fusion.2
  100.4 0.3 fusion.88
  100.7 0.2 fusion.89
  101.0 0.5 fusion.90
  101.6 0.7 add_compare_fusion.2
  102.2 0.3 fusion.88
  102.6 0.2 fusion.89
  102.8 0.6 fusion.90
  103.5 0.7 add_compare_fusion.2
  104.1 0.3 fusion.88
  104.5 0.2 fusion.89
  104.7 0.6 fusion.90
  105.3 0.7 add_compare_fusion.2
  106.0 0.3 fusion.88
  106.4 0.2 fusion.89
  106.6 0.6 fusion.90
  107.2 110.1 %all-gather.5.cloned.1.call-done = bf16[8,1024,256]{2,0,1:T(8,128)(2,1)} async-done(((bf16[8,16,256]{2,0,1:T(8,128)(2,1)}), bf16[8,1024,256]{2,0,1:T(8,128)(2,1)}) %all-gather.5.cloned.1.call-update) | async-done | bytes 4194320 | tf_op jit(solution)/shard_map/all_gather | solution.py:115
  217.3 3.3 constant_dynamic-slice_fusion.1
  220.5 1.3 copy.35
  221.9 1.4 multiply_reduce_fusion
  223.3 0.5 fusion.16
  223.8 2.4 convolution_convert_fusion
  226.3 1.0 fusion.71
  227.3 0.8 copy.34
  228.2 90.3 %all-reduce.3.cloned.1.call-done = bf16[512,2048]{1,0:T(8,128)(2,1)} async-done(((bf16[512,2048]{1,0:T(8,128)(2,1)}), bf16[512,2048]{1,0:T(8,128)(2,1)}) %all-reduce.3.cloned.1.call-update) | async-done | bytes 2097168 | tf_op jit(solution)/shard_map/psum | solution.py:130
  318.5 1.1 fusion.43
  319.6 1.8 fusion.47
  (74 shorter events, 0.7 us)
Async XLA Ops:
  7.2 216.6 %copy-start = (bf16[128,2048]{1,0:T(8,128)(2,1)S(1)}, bf16[128,2048]{1,0:T(8,128)(2,1)}, u32[]{:S(2)}) copy-start(bf16[128,2048]{1,0:T(8,128)(2,1)} %param.18) | copy-start | bytes 1572868
  7.2 55.9 %all-gather.3.cloned.1.call-start = ((), (), s32[]{:S(2)}) async-start(), calls=%async_computation | async-start | bytes 2359296 | tf_op jit(solution)/shard_map/all_gather | solution.py:69
  7.9 209.3 %all-gather.5.cloned.1.call-start = ((), (), s32[]{:S(2)}) async-start(), calls=%async_computation.1 | async-start | bytes 4259840 | tf_op jit(solution)/shard_map/all_gather | solution.py:115
  9.5 309.0 %all-reduce.3.cloned.1.call-start = ((), (), s32[]{:S(2)}) async-start(), calls=%async_computation.2 | async-start | bytes 4194304 | tf_op jit(solution)/shard_map/psum | solution.py:130
  10.2 3.0 copy-start.14
  10.2 52.8 %copy-start.6 = (bf16[2048,128]{1,0:T(8,128)(2,1)S(1)}, bf16[2048,128]{1,0:T(8,128)(2,1)}, u32[]{:S(2)}) copy-start(bf16[2048,128]{1,0:T(8,128)(2,1)} %param.15) | copy-start | bytes 1572868
  63.1 2.6 copy-start.1
  63.1 2.6 copy-start.7
  65.7 1.0 copy-start.8
  66.7 18.2 %copy-start.12 = (f32[128]{0:T(128)S(1)}, f32[128]{0:T(128)}, u32[]{:S(2)}) copy-start(f32[128]{0:T(128)} %param.20) | copy-start | bytes 1540
  66.7 18.2 %copy-start.13 = (f32[128]{0:T(128)S(1)}, f32[128]{0:T(128)}, u32[]{:S(2)}) copy-start(f32[128]{0:T(128)} %param.19) | copy-start | bytes 1540
  67.6 23.1 %copy-start.2 = (f32[512,384]{0,1:T(8,128)}, f32[512,384]{0,1:T(8,128)S(1)}, u32[]{:S(2)}) copy-start(f32[512,384]{0,1:T(8,128)S(1)} %maximum_bitcast_fusion) | copy-start | bytes 2359300
  86.2 0.6 copy-start.4
  107.2 114.7 %copy-start.5 = (bf16[512,1,64]{0,2,1:T(8,128)(2,1)S(1)}, bf16[512,1,64]{0,2,1:T(8,128)(2,1)}, u32[]{:S(2)}) copy-start(bf16[512,1,64]{0,2,1:T(8,128)(2,1)} %copy-done.4) | copy-start | bytes 196612
  226.2 1.1 copy-start.9
  226.2 1.1 copy-start.10
  226.2 93.4 %copy-start.3 = (bf16[1,64,2048]{2,1,0:T(8,128)(2,1)S(1)}, bf16[1,64,2048]{2,1,0:T(8,128)(2,1)}, u32[]{:S(2)}) copy-start(bf16[1,64,2048]{2,1,0:T(8,128)(2,1)} %param.14) | copy-start | bytes 786436
  226.2 93.4 %copy-start.11 = (f32[2048]{0:T(1024)S(1)}, f32[2048]{0:T(1024)}, u32[]{:S(2)}) copy-start(f32[2048]{0:T(1024)} %param.21) | copy-start | bytes 24580
Sparse Core Ops, SparseCore 0:
  10.1 52.9 all-gather.2
  66.9 150.2 all-gather.4
  226.4 92.0 all-reduce.2
where the time goes:
time: 329 us; the launch traced here: 328 us
  waiting for transfers between devices  248 us (75%)
  matrix products  17.8 us (5%)
  blocking collectives  17.2 us (5%)
  between operations  16.6 us (5%)
  other arithmetic  13.8 us (4%)
  local copies, waits for them, and re-layouts  13.6 us (4%)
    all_gather x1, waiting for transfers between devices, per_device(): lax.all_gather(prefix_cache, 'req', axis=1, tiled=True)  110 us
    psum x1, waiting for transfers between devices, per_device(): lax.psum(partial_out.astype(jnp.bfloat16), 'tp').astype(jnp.float32)  90.3 us
    all_gather x1, waiting for transfers between devices, per_device(): flat_rows = lax.all_gather(tokens, 'tp', axis=1, tiled=True)[0]  47.3 us
    psum x1, blocking collectives, per_device(): lax.psum((jnp.sum(queries * queries, -1), jnp.sum(keys_new * keys_new, -1...  17.2 us
    unnamed x34, local copies, waits for them, and re-layouts  7.52 us
  transfers between devices with their start and end apart: 3, of which 3 were waited for; matrix products, arithmetic and copies ran while one was open for 10% of the time, Pallas kernels for 0%

commit v1 on v0

--- a/solution.py
+++ b/solution.py
@@ -127,7 +127,9 @@
     )
     partial_out = jnp.dot(attended, w_o, preferred_element_type=jnp.float32)
     share_rows = tokens.shape[1]
-    summed = lax.psum(partial_out.astype(jnp.bfloat16), "tp").astype(jnp.float32)
+    summed = jnp.sum(lax.all_gather(partial_out.astype(jnp.bfloat16), "tp"), axis=0).astype(
+        jnp.float32
+    )
     mine = lax.dynamic_slice_in_dim(summed, lax.axis_index("tp") * share_rows, share_rows, 0)
     hidden = (tokens[0].astype(jnp.float32) + rms_scale(mine, out_gain)).astype(jnp.bfloat16)[None]
     return (hidden, appended)

time: 329 us -> 417 us (1.27)
  the two profiles are of different devices: /device:TPU:32 before, /device:TPU:1 now
where the time goes in v1:
time: 417 us; the launch traced here: 416 us
  waiting for transfers between devices  332 us (80%)
  other arithmetic  20.5 us (5%)
  matrix products  16.9 us (4%)
  between operations  16.6 us (4%)
  blocking collectives  14.7 us (4%)
  local copies, waits for them, and re-layouts  14.3 us (3%)
    all_gather x1, waiting for transfers between devices, per_device(): lax.all_gather(partial_out.astype(jnp.bfloat16), 'tp')  170 us
    all_gather x1, waiting for transfers between devices, per_device(): lax.all_gather(prefix_cache, 'req', axis=1, tiled=True)  119 us
    all_gather x1, waiting for transfers between devices, per_device(): flat_rows = lax.all_gather(tokens, 'tp', axis=1, tiled=True)[0]  42.5 us
    psum x1, blocking collectives, per_device(): lax.psum((jnp.sum(queries * queries, -1), jnp.sum(keys_new * keys_new, -1...  14.7 us
    reduce_sum x1, other arithmetic, per_device(): jnp.sum(lax.all_gather(partial_out.astype(jnp.bfloat16), 'tp'), axis=0)  9.45 us
  transfers between devices with their start and end apart: 3, of which 3 were waited for; matrix products, arithmetic and copies ran while one was open for 8% of the time, Pallas kernels for 0%

profile of v1, /device:TPU:1, one launch (start us, length us, event | category | flops | bytes accessed | tf_op | source)
XLA Modules:
  0.0 416.1 jit_solution(11173976604058768245)
XLA Ops:
  7.2 0.7 all-gather.5.cloned.1.call-update
  8.0 1.5 copy.30
  10.2 1.2 dynamic_slice.17
  12.8 3.0 copy.28
  16.4 42.5 %all-gather.5.cloned.1.call-done = bf16[1,512,2048]{2,1,0:T(8,128)(2,1)} async-done(((bf16[1,64,2048]{2,1,0:T(8,128)(2,1)}), bf16[1,512,2048]{2,1,0:T(8,128)(2,1)}) %all-gather.5.cloned.1.call-update) | async-done | bytes 2097168 | tf_op jit(solution)/shard_map/all_gather | solution.py:69
  58.9 2.6 fusion.22
  61.5 0.8 fusion.25
  62.4 0.2 copy-done.10
  62.6 0.8 fusion.19
  63.5 0.1 multiply_reduce_fusion.1
  63.5 14.7 %all-reduce = (f32[512]{0:T(512)S(1)}, f32[512]{0:T(512)S(1)}) all-reduce(f32[512]{0:T(512)S(1)} %get-tuple-element.168, f32[512]{0:T(512)S(1)} %get-tuple-element.167), channel_id=1, replica_groups=mesh['req'=64,'tp'=8] {'tp'}, use_global_device_ids=true, to_apply=%region_1.0 | all-reduce | flops 1024 | bytes 8192 | tf_op jit(solution)/shard_map/psum | solution.py:81
  78.3 0.1 multiply_bitcast_fusion
  78.4 1.3 fusion.63
  79.6 0.6 copy-done.4
  80.3 0.7 pad_maximum_fusion.2
  80.9 1.0 copy.29
  82.0 1.3 fusion.78
  83.3 0.2 fusion.39
  83.5 1.3 fusion.28
  84.7 15.0 %while.17 = (s32[]{:T(128)}, f32[1,512]{1,0:T(1,128)S(1)}, f32[1,512]{1,0:T(1,128)S(1)}, f32[1,512,128]{2,1,0:T(8,128)S(1)}, s32[]{:T(128)}, /*index=5*/bf16[409...) while((s32[]{:T(128)}, f32[1,512]{1,0:T(1,128)S(1)}, ...), condition=%wide.region_9.10_spmd, body=%wide.region_6.9_spmd.sunk | while | flops 136710144 | bytes 4622503 | solution.py:112
  84.8 0.7 add_compare_fusion.2
  85.5 0.3 fusion.88
  85.8 0.2 fusion.89
  86.1 0.6 fusion.90
  86.6 0.7 add_compare_fusion.2
  87.3 0.3 fusion.88
  87.7 0.2 fusion.89
  87.9 0.6 fusion.90
  88.5 0.7 add_compare_fusion.2
  89.2 0.3 fusion.88
  89.6 0.2 fusion.89
  89.8 0.6 fusion.90
  90.4 0.7 add_compare_fusion.2
  91.1 0.3 fusion.88
  91.5 0.2 fusion.89
  91.7 0.6 fusion.90
  92.3 0.7 add_compare_fusion.2
  93.0 0.3 fusion.88
  93.3 0.2 fusion.89
  93.6 0.6 fusion.90
  94.2 0.7 add_compare_fusion.2
  94.8 0.3 fusion.88
  95.2 0.2 fusion.89
  95.4 0.6 fusion.90
  96.0 0.7 add_compare_fusion.2
  96.7 0.3 fusion.88
  97.1 0.2 fusion.89
  97.3 0.6 fusion.90
  97.9 0.7 add_compare_fusion.2
  98.6 0.3 fusion.88
  99.0 0.2 fusion.89
  99.2 0.6 fusion.90
  99.8 119.1 %all-gather.7.cloned.1.call-done = bf16[8,1024,256]{2,0,1:T(8,128)(2,1)} async-done(((bf16[8,16,256]{2,0,1:T(8,128)(2,1)}), bf16[8,1024,256]{2,0,1:T(8,128)(2,1)}) %all-gather.7.cloned.1.call-update) | async-done | bytes 4194320 | tf_op jit(solution)/shard_map/all_gather | solution.py:115
  218.9 3.3 constant_dynamic-slice_fusion.1
  222.2 1.3 copy.35
  223.6 0.5 multiply_reduce_fusion
  224.1 0.5 fusion.16
  224.6 2.4 convolution_convert_fusion
  227.1 1.0 fusion.71
  228.2 0.8 copy.34
  229.0 170.1 %all-gather.9.cloned.1.call-done = bf16[4096,2048]{1,0:T(8,128)(2,1)} async-done(((bf16[512,2048]{1,0:T(8,128)(2,1)}), bf16[4096,2048]{1,0:T(8,128)(2,1)}) %all-gather.9.cloned.1.call-update) | async-done | bytes 16777232 | tf_op jit(solution)/shard_map/all_gather | solution.py:130
  399.1 9.5 %reduce_sum.80 = bf16[512,2048]{1,0:T(8,128)(2,1)S(1)} reduce(bf16[8,512,2048]{2,1,0:T(8,128)(2,1)} %bitcast.131, bf16[]{:T(256)} %constant.99.clone.1), dimensions={0}, to_apply=%region_12.13 | reduce | flops 7340032 | bytes 18874370 | tf_op jit(solution)/shard_map/reduce_sum | solution.py:130
  408.5 0.2 fusion.43
  408.7 0.9 fusion.47
  (77 shorter events, 0.8 us)
Async XLA Ops:
  7.2 217.5 %copy-start = (bf16[128,2048]{1,0:T(8,128)(2,1)S(1)}, bf16[128,2048]{1,0:T(8,128)(2,1)}, u32[]{:S(2)}) copy-start(bf16[128,2048]{1,0:T(8,128)(2,1)} %param.18) | copy-start | bytes 1572868
  7.2 51.8 %all-gather.5.cloned.1.call-start = ((), (), s32[]{:S(2)}) async-start(), calls=%async_computation | async-start | bytes 2359296 | tf_op jit(solution)/shard_map/all_gather | solution.py:69
  7.9 211.0 %all-gather.7.cloned.1.call-start = ((), (), s32[]{:S(2)}) async-start(), calls=%async_computation.1 | async-start | bytes 4259840 | tf_op jit(solution)/shard_map/all_gather | solution.py:115
  9.5 389.6 %all-gather.9.cloned.1.call-start = ((), (), s32[]{:S(2)}) async-start(), calls=%async_computation.2 | async-start | bytes 18874368 | tf_op jit(solution)/shard_map/all_gather | solution.py:130
  12.8 46.2 %copy-start.8 = (bf16[2048,128]{1,0:T(8,128)(2,1)S(1)}, bf16[2048,128]{1,0:T(8,128)(2,1)}, u32[]{:S(2)}) copy-start(bf16[2048,128]{1,0:T(8,128)(2,1)} %param.16) | copy-start | bytes 1572868
  58.9 2.6 copy-start.1
  58.9 2.6 copy-start.9
  61.5 1.0 copy-start.10
  62.6 15.7 %copy-start.14 = (f32[128]{0:T(128)S(1)}, f32[128]{0:T(128)}, u32[]{:S(2)}) copy-start(f32[128]{0:T(128)} %param.20) | copy-start | bytes 1540
  62.6 15.7 %copy-start.15 = (f32[128]{0:T(128)S(1)}, f32[128]{0:T(128)}, u32[]{:S(2)}) copy-start(f32[128]{0:T(128)} %param.19) | copy-start | bytes 1540
  63.5 19.8 %copy-start.2 = (f32[512,384]{0,1:T(8,128)}, f32[512,384]{0,1:T(8,128)S(1)}, u32[]{:S(2)}) copy-start(f32[512,384]{0,1:T(8,128)S(1)} %maximum_bitcast_fusion) | copy-start | bytes 2359300
  79.6 0.6 copy-start.4
  79.6 0.6 copy-start.6
  99.8 123.8 %copy-start.5 = (bf16[512,1,64]{0,2,1:T(8,128)(2,1)S(1)}, bf16[512,1,64]{0,2,1:T(8,128)(2,1)}, u32[]{:S(2)}) copy-start(bf16[512,1,64]{0,2,1:T(8,128)(2,1)} %copy-done.4) | copy-start | bytes 196612
  99.8 123.8 %copy-start.7 = (bf16[512,1,64]{0,2,1:T(8,128)(2,1)S(1)}, bf16[512,1,64]{0,2,1:T(8,128)(2,1)}, u32[]{:S(2)}) copy-start(bf16[512,1,64]{0,2,1:T(8,128)(2,1)} %copy-done.6) | copy-start | bytes 196612
  227.1 1.0 copy-start.11
  227.1 1.0 copy-start.12
  399.1 9.6 %copy-start.3 = (bf16[1,64,2048]{2,1,0:T(8,128)(2,1)S(1)}, bf16[1,64,2048]{2,1,0:T(8,128)(2,1)}, u32[]{:S(2)}) copy-start(bf16[1,64,2048]{2,1,0:T(8,128)(2,1)} %param.14) | copy-start | bytes 786436
  399.1 9.6 %copy-start.13 = (f32[2048]{0:T(1024)S(1)}, f32[2048]{0:T(1024)}, u32[]{:S(2)}) copy-start(f32[2048]{0:T(1024)} %param.21) | copy-start | bytes 24580
Sparse Core Ops, SparseCore 0:
  10.1 48.8 all-gather.4
  62.8 156.0 all-gather.6
  227.2 171.8 all-gather.8
